TPU v7x, 128 devices: a whole 4x4x4 slice. The times are simulated.
128 devices in a mesh: ctx: 16 (over x_lo, z, core), tp: 8 (over y, x_hi).
Axes of the slice: x: 4 (x_hi: 2, x_lo: 2; x = x_hi * 2 + x_lo), y: 4, z: 4, core: 2. Of those that a mesh axis runs over, the one named last changes fastest.
Arguments:
- queries: bfloat16 [8192, 4096], P('ctx', 'tp'), may hold values from -6 to 6
- key_rows: bfloat16 [8192, 4096], P('ctx', 'tp'), may hold values from -6 to 6
- value_rows: bfloat16 [8192, 4096], P('ctx', 'tp'), may hold values from -30 to 30
- selection: int32 [16, 3], replicated, may hold values from 0 to 15, as said below
- out_weight: bfloat16 [4096, 7168], P('tp'), may hold values from -0.125 to 0.125
Outputs:
- mixed: bfloat16 [8192, 7168], P('ctx', 'tp')
Inputs may be any that keep to these rules, and one draw needn't show every extreme that they name: Row q of selection lists q first, then 3 - 1 distinct blocks below q; where fewer than that lie below q, the remaining entries are q.
All inputs are finite; a program needn't handle non-finite values.
Results may differ from a plain program's by a relative error of at most 0.013.
Values may be sent and summed in bfloat16 or wider, within the bound.
No kernel may reach another device: no remote copies, remote signals or barrier semaphores. Data moves between devices by JAX's collectives and lax.ppermute only.
A program may use at most 192 MiB of HBM per device.

v0:
```python
import jax
import jax.numpy as jnp
from jax import lax
from jax.sharding import PartitionSpec as P

HD = 128
BLOCK = 512
neg_fill = -1e30


def per_device(queries, key_rows, value_rows, selection, out_weight):
    row_count, feat_width = queries.shape
    head_count = feat_width // HD
    blocks_here = row_count // BLOCK
    block_total = selection.shape[0]
    ctx_place = lax.axis_index("ctx")
    first_row = ctx_place * row_count
    scaling = 1.0 / jnp.sqrt(jnp.float32(HD))
    query_heads = queries.reshape(row_count, head_count, HD).transpose(1, 0, 2)
    own_choice = lax.dynamic_slice_in_dim(selection, ctx_place * blocks_here, blocks_here, 0)
    repeated = jnp.concatenate(
        [jnp.zeros((blocks_here, 1), bool), own_choice[:, 1:] == own_choice[:, :1]], axis=1
    )
    block_ids = jnp.arange(block_total, dtype=jnp.int32)
    chosen = jnp.any(
        (own_choice[:, :, None] == block_ids[None, None, :])
        & jnp.logical_not(repeated)[:, :, None],
        axis=1,
    )
    query_pos = first_row + jnp.arange(row_count, dtype=jnp.int32)
    initial = (
        jnp.full((head_count, row_count), neg_fill, jnp.float32),
        jnp.zeros((head_count, row_count), jnp.float32),
        jnp.zeros((head_count, row_count, HD), jnp.float32),
    )
    key_piece = lax.all_gather(key_rows, "ctx", axis=0, tiled=True)
    value_piece = lax.all_gather(value_rows, "ctx", axis=0, tiled=True)
    piece_rows = key_piece.shape[0]
    key_pos = jnp.arange(piece_rows, dtype=jnp.int32)
    in_block = (key_pos // BLOCK)[None, :] == block_ids[:, None]
    blockwise = jnp.any(chosen[:, :, None] & in_block[None, :, :], axis=1)
    allowed = jnp.broadcast_to(blockwise[:, None, :], (blocks_here, BLOCK, piece_rows)).reshape(
        row_count, piece_rows
    )
    allowed = allowed & (key_pos[None, :] <= query_pos[:, None])

    def compute(state):
        run_max, run_sum, run_acc = state
        key_heads = key_piece.reshape(piece_rows, head_count, HD).transpose(1, 0, 2)
        value_heads = value_piece.reshape(piece_rows, head_count, HD).transpose(1, 0, 2)
        scores = (
            jnp.einsum("htd,hsd->hts", query_heads, key_heads, preferred_element_type=jnp.float32)
            * scaling
        )
        new_max = jnp.maximum(run_max, jnp.max(jnp.where(allowed[None], scores, neg_fill), axis=-1))
        expo = jnp.where(allowed[None], jnp.exp(scores - new_max[..., None]), 0.0)
        new_sum = jnp.sum(expo, axis=-1)
        weights = expo.astype(jnp.bfloat16)
        new_acc = jnp.einsum(
            "hts,hsd->htd", weights, value_heads, preferred_element_type=jnp.float32
        )
        return (new_max, new_sum, new_acc)

    run_max, run_sum, run_acc = lax.cond(jnp.any(allowed), compute, lambda state: state, initial)
    attended = (
        (run_acc / run_sum[..., None])
        .astype(jnp.bfloat16)
        .transpose(1, 0, 2)
        .reshape(row_count, feat_width)
    )
    shares = lax.psum_scatter(
        lax.dot_general(
            out_weight, attended, (((0,), (1,)), ((), ())), preferred_element_type=jnp.float32
        ).astype(jnp.bfloat16),
        "tp",
        scatter_dimension=0,
        tiled=True,
    ).astype(jnp.float32)
    mixed_out = jnp.transpose(shares)
    return mixed_out.astype(jnp.bfloat16)


def solution(mesh):
    placed = (P("ctx", "tp"), P("ctx", "tp"), P("ctx", "tp"), P(), P("tp", None))
    return jax.shard_map(
        per_device, mesh=mesh, in_specs=placed, out_specs=P("ctx", "tp"), check_vma=False
    )
```

profile of v0, /device:TPU:1, one launch (start us, length us, event | category | flops | bytes accessed | tf_op | source)
XLA Modules:
  0.0 339.7 jit_solution(13768091969145868570)
XLA Ops:
  6.5 0.0 all-gather.3.cloned.1.call-start
  6.5 0.7 all-gather.3.cloned.1.call-update
  7.3 0.0 all-gather.5.cloned.1.call-start
  7.3 0.7 all-gather.5.cloned.1.call-update
  8.0 0.0 reduce-scatter.4.cloned.1.call-start
  8.1 0.9 fusion.20
  8.9 0.5 slice.7
  9.4 1.3 copy.20
  10.7 0.8 compare_reduce_fusion
  11.5 0.1 add_not_fusion
  11.6 0.1 fusion.18
  11.6 0.2 fusion.13
  11.8 7.3 %fusion.10 = (pred[512,8192]{1,0:T(8,128)(4,1)}, pred[]{:T(512)}) fusion(s32[512]{0:T(512)S(1)} %iota_add_fusion, pred[8192]{0:T(1024)(128)(4,1)S(1)} %fusion.13), kind=kLoop, calls=%fused_computation.15 | loop fusion | flops 12582911 | bytes 4204545 | tf_op jit(solution)/shard_map/and | solution.py:45
  19.8 45.1 %all-gather.3.cloned.1.call-done = bf16[8192,512]{1,0:T(8,128)(2,1)} async-done(((bf16[512,512]{1,0:T(8,128)(2,1)}), bf16[8192,512]{1,0:T(8,128)(2,1)}) %all-gather.3.cloned.1.call-update) | async-done | bytes 8388624 | tf_op jit(solution)/shard_map/all_gather | solution.py:36
  64.9 54.9 %all-gather.5.cloned.1.call-done = bf16[8192,512]{1,0:T(8,128)(2,1)} async-done(((bf16[512,512]{1,0:T(8,128)(2,1)}), bf16[8192,512]{1,0:T(8,128)(2,1)}) %all-gather.5.cloned.1.call-update) | async-done | bytes 8388624 | tf_op jit(solution)/shard_map/all_gather | solution.py:37
  119.8 84.5 %conditional.1 = (f32[4,512]{1,0:T(4,128)S(1)}, f32[4,512,128]{1,2,0:T(8,128)S(1)}) conditional(s32[]{:T(128)} %convert_element_type.20, () %tuple.13, (pred[512,8192]{1,0:T(8,128)(4,1)}, bf16[8192,512]{1,0:T(8,128)(2,1)}, bf16[4,512,128]{1,2,0:T(8,128)(2,1)S(1)}, bf16[8192,512]{1,0:T(8,128)(2,1)}) %tuple.31), branch_computations={%region_3.4_spmd, %region_4.7_spmd} | conditional | flops 8774481920 | bytes 232308752 | solution.py:64
  119.8 29.7 %select_reduce_fusion = (f32[4,512]{1,0:T(4,128)S(1)}, f32[4,512,8192]{2,1,0:T(8,128)}) fusion(pred[512,8192]{1,0:T(8,128)(4,1)} %get-tuple-element.13, bf16[4,512,128]{1,2,0:T(8,128)(2,1)S(1)} %get-tuple-element.31, bf16[8192,512]{1,0:T(8,128)(2,1)} %get-tuple-element.15), kind=kOutput, calls=%fused_computation.1 | convolution fusion | flops 4345296896 | bytes 80224256 | tf_op jit(solution)/shard_map/cond/branch_1_fun/htd,hsd->hts/dot_general | solution.py:52
  149.5 31.8 %fusion.2 = f32[4,512,128]{1,2,0:T(8,128)S(1)} fusion(f32[4,512,8192]{2,1,0:T(8,128)} %get-tuple-element.37, f32[4,512]{1,0:T(4,128)S(1)} %broadcast_maximum_fusion, pred[512,8192]{1,0:T(8,128)(4,1)} %get-tuple-element.13, bf16[8192,512]{1,0:T(8,128)(2,1)} %get-tuple-element.16), kind=kOutput, calls=%fused_computation.4 | convolution fusion | flops 4362076160 | bytes 80748544 | tf_op jit(solution)/shard_map/cond | solution.py:64
  181.3 22.7 %fusion.1 = f32[4,512]{1,0:T(4,128)S(1)} fusion(f32[4,512,8192]{2,1,0:T(8,128)} %get-tuple-element.37, f32[4,512]{1,0:T(4,128)S(1)} %broadcast_maximum_fusion, pred[512,8192]{1,0:T(8,128)(4,1)} %get-tuple-element.13), kind=kLoop, calls=%fused_computation.3 | loop fusion | flops 67106816 | bytes 71319552 | tf_op jit(solution)/shard_map/cond/branch_1_fun/reduce_sum | solution.py:57
  204.2 0.1 divide_convert_fusion
  204.4 9.2 %fusion.11 = bf16[7168,512]{0,1:T(8,128)(2,1)} fusion(bf16[512,512]{0,1:T(8,128)(2,1)S(1)} %bitcast.38, bf16[512,7168]{1,0:T(8,128)(2,1)} %param.11), kind=kOutput, calls=%fused_computation.17 | convolution fusion | flops 3761766400 | bytes 15204352 | tf_op jit(solution)/shard_map/dot_general | solution.py:72
  213.6 10.4 %copy.24 = bf16[7168,512]{1,0:T(8,128)(2,1)} copy(bf16[7168,512]{0,1:T(8,128)(2,1)} %fusion.11) | data formatting | bytes 14680064
  224.0 0.0 reduce-scatter.4.cloned.1.call-update
  224.0 106.9 %reduce-scatter.4.cloned.1.call-done = bf16[896,512]{1,0:T(8,128)(2,1)} async-done(((bf16[7168,512]{1,0:T(8,128)(2,1)}), bf16[896,512]{1,0:T(8,128)(2,1)}) %reduce-scatter.4.cloned.1.call-update) | async-done | bytes 917520
  330.9 2.2 copy.25
  (3 shorter events, 0.0 us)
Async XLA Ops:
  6.5 58.4 %all-gather.3.cloned.1.call-start = ((), (), s32[]{:S(2)}) async-start(), calls=%async_computation.1 | async-start | bytes 8912896 | tf_op jit(solution)/shard_map/all_gather | solution.py:36
  7.3 112.5 %all-gather.5.cloned.1.call-start = ((), (), s32[]{:S(2)}) async-start(), calls=%async_computation.2 | async-start | bytes 8912896 | tf_op jit(solution)/shard_map/all_gather | solution.py:37
  8.0 322.9 %reduce-scatter.4.cloned.1.call-start = ((), (), s32[]{:S(2)}) async-start(), calls=%async_computation.3 | async-start | bytes 8257536
Sparse Core Ops, SparseCore 0:
  9.1 55.7 all-gather.2
  66.6 53.1 all-gather.4
  224.2 106.7 reduce-scatter.3
where the time goes:
time: 340 us
  waiting for transfers between devices  208 us (61%)
  matrix products  70.8 us (21%)
  other arithmetic  31.3 us (9%)
  local copies, waits for them, and re-layouts  15.3 us (4%)
  between operations  13.8 us (4%)
    unnamed x4, waiting for transfers between devices  108 us
    all_gather x1, waiting for transfers between devices, per_device(): value_piece = lax.all_gather(value_rows, 'ctx', axis=0, tiled=True)  54.9 us
    all_gather x1, waiting for transfers between devices, per_device(): key_piece = lax.all_gather(key_rows, 'ctx', axis=0, tiled=True)  45.1 us
    cond x1, matrix products, per_device(): lax.cond(jnp.any(allowed), compute, lambda state: state, initial)  31.8 us
    dot_general x1, matrix products, compute(): jnp.einsum('htd,hsd->hts', query_heads, key_heads, preferred_element_type...  29.7 us
    reduce_sum x1, other arithmetic, compute(): new_sum = jnp.sum(expo, axis=-1)  22.7 us
    unnamed x3, local copies, waits for them, and re-layouts  13.9 us
    dot_general x1, matrix products, per_device(): lax.dot_general(out_weight, attended, (((0,), (1,)), ((), ())), preferred...  9.24 us
  transfers between devices with their start and end apart: 3, of which 3 were waited for; matrix products, arithmetic and copies ran while one was open for 3% of the time, Pallas kernels for 0%

commit v1 on v0

--- a/solution.py
+++ b/solution.py
@@ -34,7 +34,15 @@
         jnp.zeros((head_count, row_count, HD), jnp.float32),
     )
     key_piece = lax.all_gather(key_rows, "ctx", axis=0, tiled=True)
-    value_piece = lax.all_gather(value_rows, "ctx", axis=0, tiled=True)
+    value_piece = jnp.concatenate(
+        lax.all_to_all(
+            jnp.stack(lax.axis_size("ctx") * [value_rows], axis=0),
+            "ctx",
+            split_axis=0,
+            concat_axis=0,
+        ),
+        axis=0,
+    )
     piece_rows = key_piece.shape[0]
     key_pos = jnp.arange(piece_rows, dtype=jnp.int32)
     in_block = (key_pos // BLOCK)[None, :] == block_ids[:, None]

time: 340 us -> 404 us (1.19)
  waiting for transfers between devices: 208 us -> 246 us
  local copies, waits for them, and re-layouts: 15.3 us -> 31.1 us
  starting transfers between devices: 0.08 us -> 7.8 us
    all_to_all x0 -> x1, waiting for transfers between devices: none -> 137 us  [per_device(): lax.all_to_all(jnp.stack(lax.axis_size('ctx') * [value_rows], axis=0), 'c...]
    all_gather x1 -> x0, waiting for transfers between devices: 54.9 us -> none  [per_device(): value_piece = lax.all_gather(value_rows, 'ctx', axis=0, tiled=True)]
    all_gather x1, waiting for transfers between devices: 45.1 us -> 0.01 us  [per_device(): key_piece = lax.all_gather(key_rows, 'ctx', axis=0, tiled=True)]
    another operation x0 -> x2, local copies, waits for them, and re-layouts: none -> 17.6 us  [the longest x1 12.5 us: compute(): value_piece.reshape(piece_rows, head_count, HD).transpose(1, 0, 2)]
    all_to_all x0 -> x1, starting transfers between devices: none -> 7.76 us  [per_device(): lax.all_to_all(jnp.stack(lax.axis_size('ctx') * [value_rows], axis=0), 'c...]
    unnamed x3 -> x7, local copies, waits for them, and re-layouts: 13.9 us -> 12.8 us
    unnamed x4 -> x3, waiting for transfers between devices: 108 us -> 109 us
  transfers between devices with their start and end apart: 3 -> 3, of which waited for: 3 -> 2; matrix products, arithmetic and copies ran while one was open for 3% -> 4% of each run, Pallas kernels for 0% -> 0%
where the time goes in v1:
time: 404 us; the launch traced here: 403 us
  waiting for transfers between devices  246 us (61%)
  matrix products  72.1 us (18%)
  other arithmetic  31.4 us (8%)
  local copies, waits for them, and re-layouts  31.1 us (8%)
  between operations  14.1 us (3%)
  starting transfers between devices  7.8 us (2%)
    all_to_all x1, waiting for transfers between devices, per_device(): lax.all_to_all(jnp.stack(lax.axis_size('ctx') * [value_rows], axis=0), 'c...  137 us
    unnamed x3, waiting for transfers between devices  109 us
    cond x1, matrix products, per_device(): lax.cond(jnp.any(allowed), compute, lambda state: state, initial)  33.2 us
    dot_general x1, matrix products, compute(): jnp.einsum('htd,hsd->hts', query_heads, key_heads, preferred_element_type...  29.7 us
    reduce_sum x1, other arithmetic, compute(): new_sum = jnp.sum(expo, axis=-1)  22.9 us
    unnamed x7, local copies, waits for them, and re-layouts  12.8 us
    another operation x1, local copies, waits for them, and re-layouts, compute(): value_piece.reshape(piece_rows, head_count, HD).transpose(1, 0, 2)  12.5 us
    dot_general x1, matrix products, per_device(): lax.dot_general(out_weight, attended, (((0,), (1,)), ((), ())), preferred...  9.24 us
  transfers between devices with their start and end apart: 3, of which 2 were waited for; matrix products, arithmetic and copies ran while one was open for 4% of the time, Pallas kernels for 0%

profile of v1, /device:TPU:1, one launch (start us, length us, event | category | flops | bytes accessed | tf_op | source)
XLA Modules:
  0.0 402.7 jit_solution(17212824046103471834)
XLA Ops:
  6.5 0.0 copy-start.1
  6.5 0.0 copy-start
  6.5 0.0 all-gather.2.cloned.1.call-start
  6.5 0.7 all-gather.2.cloned.1.call-update
  7.3 5.1 %stack.2 = bf16[16,512,512]{2,1,0:T(8,128)(2,1)} broadcast(bf16[512,512]{1,0:T(8,128)(2,1)} %param.9), dimensions={1,2} | broadcast | bytes 8912896 | tf_op jit(solution)/shard_map/stack | solution.py:39
  12.3 7.8 %all-to-all-start = ((bf16[16,512,512]{2,1,0:T(8,128)(2,1)}), bf16[16,512,512]{2,1,0:T(8,128)(2,1)}, u32[]{:S(2)}, u32[]{:S(2)}) async-start(bf16[16,512,512]{2,1,0:T(8,128)(2,1)} %stack.2), calls=%async_computation | async-start | bytes 16777216 | tf_op jit(solution)/shard_map/all_to_all | solution.py:38
  20.1 0.0 reduce-scatter.4.cloned.1.call-start
  20.1 0.0 copy-done.1
  20.2 0.2 fusion.21
  20.3 0.5 slice.7
  20.9 0.0 copy-done
  20.9 0.2 copy.20
  21.1 0.8 compare_reduce_fusion
  21.9 0.1 add_not_fusion
  21.9 0.1 fusion.19
  22.0 0.2 fusion.14
  22.2 7.3 %fusion.11 = (pred[512,8192]{1,0:T(8,128)(4,1)}, pred[]{:T(512)}) fusion(s32[512]{0:T(512)S(1)} %iota_add_fusion, pred[8192]{0:T(1024)(128)(4,1)S(1)} %fusion.14), kind=kLoop, calls=%fused_computation.15 | loop fusion | flops 12582911 | bytes 4204545 | tf_op jit(solution)/shard_map/and | solution.py:53
  30.2 136.7 %all-to-all-done = bf16[16,512,512]{2,1,0:T(8,128)(2,1)} async-done(((bf16[16,512,512]{2,1,0:T(8,128)(2,1)}), bf16[16,512,512]{2,1,0:T(8,128)(2,1)}, u32[]{:S(2)}, u32[]{:S(2)}) %all-to-all-start) | async-done | bytes 8388640 | tf_op jit(solution)/shard_map/all_to_all | solution.py:38
  166.9 0.0 all-gather.2.cloned.1.call-done
  166.9 98.4 %conditional.1 = (f32[4,512]{1,0:T(4,128)S(1)}, f32[4,512,128]{1,2,0:T(8,128)S(1)}) conditional(s32[]{:T(128)} %convert_element_type.20, () %tuple.13, (pred[512,8192]{1,0:T(8,128)(4,1)}, bf16[8192,512]{1,0:T(8,128)(2,1)}, bf16[4,512,128]{1,2,0:T(8,128)(2,1)S(1)}, bf16[16,512,512]{2,1,0:T(8,128)(2,1)}) %tuple.29), branch_computations={%region_3.4_spmd, %region_4.7_spmd} | conditional | flops 8774481920 | bytes 249085968 | solution.py:72
  166.9 12.5 %reshape_reshape.2 = bf16[8192,4,128]{2,1,0:T(4,128)(2,1)} reshape(bf16[16,512,512]{2,1,0:T(8,128)(2,1)} %get-tuple-element.16) | data formatting | bytes 16777216 | tf_op jit(solution)/shard_map/cond/branch_1_fun/reshape;reshape | solution.py:58
  179.4 29.7 %select_reduce_fusion = (f32[4,512]{1,0:T(4,128)S(1)}, f32[4,512,8192]{2,1,0:T(8,128)}) fusion(pred[512,8192]{1,0:T(8,128)(4,1)} %get-tuple-element.13, bf16[4,512,128]{1,2,0:T(8,128)(2,1)S(1)} %get-tuple-element.31, bf16[8192,512]{1,0:T(8,128)(2,1)} %get-tuple-element.15), kind=kOutput, calls=%fused_computation.1 | convolution fusion | flops 4345296896 | bytes 80224256 | tf_op jit(solution)/shard_map/cond/branch_1_fun/htd,hsd->hts/dot_general | solution.py:60
  209.1 33.2 %fusion.2 = f32[4,512,128]{1,2,0:T(8,128)S(1)} fusion(f32[4,512,8192]{2,1,0:T(8,128)} %get-tuple-element.37, f32[4,512]{1,0:T(4,128)S(1)} %broadcast_maximum_fusion, pred[512,8192]{1,0:T(8,128)(4,1)} %get-tuple-element.13, bf16[8192,4,128]{2,1,0:T(4,128)(2,1)} %reshape_reshape.2), kind=kOutput, calls=%fused_computation.4 | convolution fusion | flops 4362076160 | bytes 80748544 | tf_op jit(solution)/shard_map/cond | solution.py:72
  242.3 22.9 %fusion.1 = f32[4,512]{1,0:T(4,128)S(1)} fusion(f32[4,512,8192]{2,1,0:T(8,128)} %get-tuple-element.37, f32[4,512]{1,0:T(4,128)S(1)} %broadcast_maximum_fusion, pred[512,8192]{1,0:T(8,128)(4,1)} %get-tuple-element.13), kind=kLoop, calls=%fused_computation.3 | loop fusion | flops 67106816 | bytes 71319552 | tf_op jit(solution)/shard_map/cond/branch_1_fun/reduce_sum | solution.py:65
  265.3 0.1 divide_convert_fusion
  265.5 9.2 %fusion.12 = bf16[7168,512]{0,1:T(8,128)(2,1)} fusion(bf16[512,512]{0,1:T(8,128)(2,1)S(1)} %bitcast.31, bf16[512,7168]{1,0:T(8,128)(2,1)} %param.11), kind=kOutput, calls=%fused_computation.17 | convolution fusion | flops 3761766400 | bytes 15204352 | tf_op jit(solution)/shard_map/dot_general | solution.py:80
  274.7 10.4 %copy.24 = bf16[7168,512]{1,0:T(8,128)(2,1)} copy(bf16[7168,512]{0,1:T(8,128)(2,1)} %fusion.12) | data formatting | bytes 14680064
  285.1 0.0 reduce-scatter.4.cloned.1.call-update
  285.1 108.6 %reduce-scatter.4.cloned.1.call-done = bf16[896,512]{1,0:T(8,128)(2,1)} async-done(((bf16[7168,512]{1,0:T(8,128)(2,1)}), bf16[896,512]{1,0:T(8,128)(2,1)}) %reduce-scatter.4.cloned.1.call-update) | async-done | bytes 917520
  393.7 2.2 copy.25
  (3 shorter events, 0.0 us)
Async XLA Ops:
  6.5 13.6 %copy-start.1 = (s32[16,3]{0,1:T(4,128)S(1)}, s32[16,3]{0,1:T(4,128)}, u32[]{:S(2)}) copy-start(s32[16,3]{0,1:T(4,128)} %param.10) | copy-start | bytes 580
  6.5 14.3 %copy-start = (bf16[512,512]{1,0:T(8,128)(2,1)S(1)}, bf16[512,512]{1,0:T(8,128)(2,1)}, u32[]{:S(2)}) copy-start(bf16[512,512]{1,0:T(8,128)(2,1)} %param.7) | copy-start | bytes 1572868
  6.5 160.3 %all-gather.2.cloned.1.call-start = ((), (), s32[]{:S(2)}) async-start(), calls=%async_computation.2 | async-start | bytes 8912896 | tf_op jit(solution)/shard_map/all_gather | solution.py:36
  12.3 154.5 %all-to-all-start = ((bf16[16,512,512]{2,1,0:T(8,128)(2,1)}), bf16[16,512,512]{2,1,0:T(8,128)(2,1)}, u32[]{:S(2)}, u32[]{:S(2)}) async-start(bf16[16,512,512]{2,1,0:T(8,128)(2,1)} %stack.2), calls=%async_computation | async-start | bytes 16777216 | tf_op jit(solution)/shard_map/all_to_all | solution.py:38
  20.1 373.6 %reduce-scatter.4.cloned.1.call-start = ((), (), s32[]{:S(2)}) async-start(), calls=%async_computation.3 | async-start | bytes 8257536
Sparse Core Ops, SparseCore 0:
  9.1 147.3 all-gather.1
  285.3 108.3 reduce-scatter.3
